TPU v7x, 256 devices: a whole 4x4x8 slice. The times are simulated.
256 devices in a mesh: gx: 32 (over z_lo, y, core), gy: 4 (over x), gz: 2 (over z_hi).
Axes of the slice: x: 4, y: 4, z: 8 (z_hi: 2, z_lo: 4; z = z_hi * 4 + z_lo), core: 2. Of those that a mesh axis runs over, the one named last changes fastest.
Arguments:
- f_pop: float32 [19, 128, 64, 256], P(None, 'gx', 'gy', 'gz'), may hold values from 0.02 to 0.1
- g_pop: float32 [19, 128, 64, 256], P(None, 'gx', 'gy', 'gz'), may hold values from -0.2 to 0.2
- displacement: int32 [1], replicated, may hold values from 33 to 47
Outputs:
- f_new: float32 [19, 128, 64, 256], P(None, 'gx', 'gy', 'gz')
- g_new: float32 [19, 128, 64, 256], P(None, 'gx', 'gy', 'gz')
All inputs are finite; a program needn't handle non-finite values.
Results may differ from a plain program's by a relative error of at most 0.0001.
Values sent between devices are 32-bit elements; how exact they have to be, the bound alone decides.
No kernel may reach another device: no remote copies, remote signals or barrier semaphores. Data moves between devices by JAX's collectives and lax.ppermute only.
A program may use at most 64 MiB of HBM per device.

v0:
```python
import jax
import jax.numpy as jnp
from jax import lax
from jax.sharding import PartitionSpec as P

VELOCITIES = [
    (0, 0, 0),
    (1, 0, 0),
    (1, 1, 0),
    (1, -1, 0),
    (1, 0, 1),
    (1, 0, -1),
    (-1, 0, 0),
    (-1, -1, 0),
    (-1, 1, 0),
    (-1, 0, -1),
    (-1, 0, 1),
    (0, 1, 0),
    (0, -1, 0),
    (0, 0, 1),
    (0, 0, -1),
    (0, 1, 1),
    (0, -1, -1),
    (0, 1, -1),
    (0, -1, 1),
]
BULK_COEF = 0.5
STIFFNESS = 0.5
TAU_FLUID = 0.8
TAU_ORDER = 0.9


def with_halo(cells, sides, width):
    for axis, dim in sides:
        count = lax.axis_size(axis)
        head = lax.slice_in_dim(cells, 0, width, axis=dim)
        tail = lax.slice_in_dim(cells, cells.shape[dim] - width, cells.shape[dim], axis=dim)
        cells = jnp.concatenate(
            [
                lax.ppermute(tail, axis, [(i, (i + 1) % count) for i in range(count)]),
                cells,
                lax.ppermute(head, axis, [((i + 1) % count, i) for i in range(count)]),
            ],
            axis=dim,
        )
    return cells


def lattice_weight(number):
    steps_sq = sum((abs(comp) for comp in VELOCITIES[number]))
    if steps_sq == 0:
        return 1.0 / 3.0
    if steps_sq == 1:
        return 1.0 / 18.0
    return 1.0 / 36.0


def along(number, values, base):
    result = jnp.zeros_like(base)
    for axis_id in range(3):
        comp = VELOCITIES[number][axis_id]
        if comp != 0:
            result = result + comp * values[axis_id]
    return result


def collide(f_pop, g_pop, order_field, laplace, slopes):
    density = jnp.sum(f_pop, axis=0)
    chemical = (
        BULK_COEF * (order_field * order_field * order_field - order_field) - STIFFNESS * laplace
    )
    forces = [chemical * slope for slope in slopes]
    moments = []
    for axis_id in range(3):
        moment = jnp.zeros_like(density)
        for number in range(19):
            comp = VELOCITIES[number][axis_id]
            if comp != 0:
                moment = moment + comp * f_pop[number]
        moments.append(moment)
    flows = [(moments[axis_id] + 0.5 * forces[axis_id]) / density for axis_id in range(3)]
    speed_sq = flows[0] * flows[0] + flows[1] * flows[1] + flows[2] * flows[2]
    flow_force = flows[0] * forces[0] + flows[1] * forces[1] + flows[2] * forces[2]
    f_posts = []
    g_eqs = []
    for number in range(19):
        weight = lattice_weight(number)
        proj_flow = along(number, flows, density)
        proj_force = along(number, forces, density)
        shape_term = 3.0 * proj_flow + 4.5 * proj_flow * proj_flow - 1.5 * speed_sq
        f_eq = weight * density * (1.0 + shape_term)
        source = (
            (1.0 - 0.5 / TAU_FLUID)
            * weight
            * (3.0 * (proj_force - flow_force) + 9.0 * proj_flow * proj_force)
        )
        f_posts.append(f_pop[number] - (f_pop[number] - f_eq) / TAU_FLUID + source)
        g_eqs.append(weight * (3.0 * chemical + order_field * shape_term))
    rest_eq = order_field
    for number in range(1, 19):
        rest_eq = rest_eq - g_eqs[number]
    g_eqs[0] = rest_eq
    g_posts = [g_pop[number] - (g_pop[number] - g_eqs[number]) / TAU_ORDER for number in range(19)]
    return (jnp.stack(f_posts), jnp.stack(g_posts))


def window(whole, begin, rows, whole_rows):
    begin = jnp.mod(begin, whole_rows)
    doubled = jnp.concatenate([whole, whole], axis=1)
    return lax.dynamic_slice_in_dim(doubled, begin, rows, 1)


def sliding(edges, shift):
    extended = with_halo(edges, (("gx", 1),), 1)
    below = extended[:, 0]
    above = extended[:, 3]
    whole_below, whole_above = (
        lax.all_gather(below, "gy", axis=1, tiled=True),
        lax.all_gather(above, "gy", axis=1, tiled=True),
    )
    rows = below.shape[1]
    whole_rows = whole_below.shape[1]
    start = lax.axis_index("gy") * rows
    return (
        window(whole_below, start - shift, rows, whole_rows),
        window(whole_above, start + shift, rows, whole_rows),
    )


def extend_x(posts, below, above):
    rows, layers = (posts.shape[2], posts.shape[3])
    lower = jnp.concatenate(
        [
            jnp.zeros((1, rows, layers), jnp.float32),
            below,
            jnp.zeros((13, rows, layers), jnp.float32),
        ],
        axis=0,
    )
    upper = jnp.concatenate(
        [
            jnp.zeros((6, rows, layers), jnp.float32),
            above,
            jnp.zeros((8, rows, layers), jnp.float32),
        ],
        axis=0,
    )
    return jnp.concatenate([lower[:, None], posts, upper[:, None]], axis=1)


def local(f_pop, g_pop, displacement):
    shift = displacement[0]
    width_x, width_y, width_z = (f_pop.shape[1], f_pop.shape[2], f_pop.shape[3])
    order_field = jnp.sum(g_pop, axis=0)
    phase_edges = jnp.stack([order_field[0], order_field[-1]])[None]
    phase_below, phase_above = sliding(phase_edges, shift)
    neigh_xm = jnp.concatenate([phase_below, order_field[:-1]], axis=0)
    neigh_xp = jnp.concatenate([order_field[1:], phase_above], axis=0)
    padded = with_halo(order_field, (("gy", 1), ("gz", 2)), 1)
    neigh_ym = padded[:, :-2, 1:-1]
    neigh_yp = padded[:, 2:, 1:-1]
    neigh_zm = padded[:, 1:-1, :-2]
    neigh_zp = padded[:, 1:-1, 2:]
    laplace = neigh_xm + neigh_xp + neigh_ym + neigh_yp + neigh_zm + neigh_zp - 6.0 * order_field
    slopes = [0.5 * (neigh_xp - neigh_xm), 0.5 * (neigh_yp - neigh_ym), 0.5 * (neigh_zp - neigh_zm)]
    f_post, g_post = collide(f_pop, g_pop, order_field, laplace, slopes)
    pop_edges = jnp.concatenate(
        [
            jnp.stack([f_post[6:11, 0], f_post[1:6, -1]], axis=1),
            jnp.stack([g_post[6:11, 0], g_post[1:6, -1]], axis=1),
        ],
        axis=0,
    )
    pop_below, pop_above = sliding(pop_edges, shift)
    layered = jnp.concatenate(
        [
            extend_x(f_post, pop_below[0:5], pop_above[0:5]),
            extend_x(g_post, pop_below[5:10], pop_above[5:10]),
        ],
        axis=0,
    )
    results = []
    padded_all = with_halo(layered, (("gy", 2), ("gz", 3)), 1)
    for number in range(38):
        vel_x, vel_y, vel_z = VELOCITIES[number % 19]
        results.append(
            padded_all[
                number,
                1 - vel_x : 1 - vel_x + width_x,
                1 - vel_y : 1 - vel_y + width_y,
                1 - vel_z : 1 - vel_z + width_z,
            ]
        )
    f_new = jnp.stack(results[:19])
    g_new = jnp.stack(results[19:])
    return (f_new, g_new)


def solution(mesh):
    return jax.shard_map(
        local,
        mesh=mesh,
        in_specs=(P(None, "gx", "gy", "gz"), P(None, "gx", "gy", "gz"), P()),
        out_specs=(P(None, "gx", "gy", "gz"), P(None, "gx", "gy", "gz")),
        check_vma=False,
    )
```

profile of v0, /device:TPU:6, one launch (start us, length us, event | category | flops | bytes accessed | tf_op | source)
XLA Modules:
  0.0 120.2 jit_solution(16818710644719364818)
XLA Ops:
  0.7 1.2 %reduce_sum.19 = f32[4,16,128]{2,1,0:T(8,128)S(1)} reduce(f32[19,4,16,128]{3,2,1,0:T(8,128)} %param.4, f32[]{:T(128)} %constant.95.clone.1), dimensions={0}, to_apply=%region_1.2 | reduce | flops 147456 | bytes 655364 | tf_op jit(solution)/shard_map/reduce_sum | solution.py:154
  1.9 0.9 collective-permute-start.3
  2.8 2.4 %collective-permute-start.2 = (f32[4,1,128]{2,1,0:T(1,128)S(1)}, f32[4,1,128]{2,1,0:T(1,128)S(1)}, u32[]{:S(2)}, u32[]{:S(2)}) collective-permute-start(f32[4,1,128]{2,1,0:T(1,128)S(1)} %get-tuple-element.109), channel_id=1, source_target_pairs={{0,2},{2,4},{4,6},{6,0},{1,3},{3,5},{5,7},{7,1},{8,10},{10,12},{12... | collective-permute-start | bytes 6152 | tf_op jit(solution)/shard_map/ppermute | solution.py:40
  5.2 6.0 %collective-permute-start.1 = (f32[1,1,16,128]{3,2,1,0:T(8,128)S(1)}, f32[1,1,16,128]{3,2,1,0:T(8,128)S(1)}, u32[]{:S(2)}, u32[]{:S(2)}) collective-permute-start(f32[1,1,16,128]{3,2,1,0:T(8,128)S(1)} %get-tuple-element.114), channel_id=1, source_target_pairs={{8,0},{16,8},{24,16},{32,24},{40,32},{48,40},{56,48},{64,56},{72,6... | collective-permute-start | bytes 24584 | tf_op jit(solution)/shard_map/ppermute | solution.py:42
  12.1 1.1 reduce_sum.18
  13.4 4.5 %collective-permute-start.5 = (f32[4,18,1]{2,1,0:T(8,128)S(1)}, f32[4,18,1]{2,1,0:T(8,128)S(1)}, u32[]{:S(2)}, u32[]{:S(2)}) collective-permute-start(f32[4,18,1]{2,1,0:T(8,128)S(1)} %get-tuple-element.106), channel_id=1, source_target_pairs={{1,0},{0,1},{3,2},{2,3},{5,4},{4,5},{7,6},{6,7},{9,8},{8,9},{11,10... | collective-permute-start | bytes 872 | tf_op jit(solution)/shard_map/ppermute | solution.py:42
  17.9 1.4 %collective-permute-start.4 = (f32[4,18,1]{2,1,0:T(8,128)S(1)}, f32[4,18,1]{2,1,0:T(8,128)S(1)}, u32[]{:S(2)}, u32[]{:S(2)}) collective-permute-start(f32[4,18,1]{2,1,0:T(8,128)S(1)} %get-tuple-element.107), channel_id=1, source_target_pairs={{0,1},{1,0},{2,3},{3,2},{4,5},{5,4},{6,7},{7,6},{8,9},{9,8},{10,11... | collective-permute-start | bytes 872 | tf_op jit(solution)/shard_map/ppermute | solution.py:40
  19.4 11.9 %all-gather = f32[1,1,64,128]{3,2,1,0:T(8,128)S(1)} all-gather(f32[1,1,16,128]{3,2,1,0:T(8,128)S(1)} %collective-permute-done), channel_id=2, replica_groups=mesh['gx'=32,'gy'=4,'gz'=2] {'gy'}, dimensions={2}, use_global_device_ids=true | all-gather | bytes 40960 | tf_op jit(solution)/shard_map/all_gather | solution.py:118
  31.3 11.9 %all-gather.1 = f32[1,1,64,128]{3,2,1,0:T(8,128)S(1)} all-gather(f32[1,1,16,128]{3,2,1,0:T(8,128)S(1)} %collective-permute-done.1), channel_id=3, replica_groups=mesh['gx'=32,'gy'=4,'gz'=2] {'gy'}, dimensions={2}, use_global_device_ids=true | all-gather | bytes 40960 | tf_op jit(solution)/shard_map/all_gather | solution.py:119
  43.2 1.4 %bitcast_subtract_fusion.16 = (f32[4,16,128]{2,1,0:T(8,128)S(1)}, f32[4,16,128]{2,1,0:T(8,128)S(1)}, f32[4,16,128]{2,1,0:T(8,128)S(1)}, f32[4,16,128]{2,1,0:T(8,...) fusion(f32[4,16,128]{2,1,0:T(8,128)S(1)} %reduce_sum.19, ...), kind=kLoop, calls=%fused_computation.190 | loop fusion | flops 2064384 | bytes 1512000 | tf_op jit(solution)/shard_map/sub | solution.py:103
  45.5 0.5 collective-permute-start.6
  46.0 0.8 copy.371
  47.3 6.0 %collective-permute-done.6 = f32[10,1,16,128]{3,2,1,0:T(8,128)S(1)} collective-permute-done((f32[10,1,16,128]{3,2,1,0:T(8,128)S(1)}, f32[10,1,16,128]{3,2,1,0:T(8,128)S(1)}, u32[]{:S(2)}, u32[]{:S(2)}) %collective-permute-start.6) | collective-permute-done | bytes 81952 | tf_op jit(solution)/shard_map/ppermute | solution.py:40
  53.4 12.4 %all-gather.2 = f32[10,1,64,128]{3,1,0,2:T(1,128)S(1)} all-gather(f32[10,1,16,128]{3,1,0,2:T(1,128)S(1)} %copy.282), channel_id=4, replica_groups=mesh['gx'=32,'gy'=4,'gz'=2] {'gy'}, dimensions={2}, use_global_device_ids=true | all-gather | bytes 409600 | tf_op jit(solution)/shard_map/all_gather | solution.py:118
  66.0 12.4 %all-gather.3 = f32[10,1,64,128]{3,1,0,2:T(1,128)S(1)} all-gather(f32[10,1,16,128]{3,1,0,2:T(1,128)S(1)} %copy.284), channel_id=5, replica_groups=mesh['gx'=32,'gy'=4,'gz'=2] {'gy'}, dimensions={2}, use_global_device_ids=true | all-gather | bytes 409600 | tf_op jit(solution)/shard_map/all_gather | solution.py:119
  78.5 0.1 maximum_bitcast_fusion.2
  78.6 0.1 maximum_bitcast_fusion.1
  78.7 0.2 fusion
  78.9 0.7 collective-permute-start.8
  79.6 1.7 %collective-permute-start.9 = (f32[38,6,1,128]{3,0,2,1:T(8,128)S(1)}, f32[38,6,1,128]{3,0,2,1:T(8,128)S(1)}, u32[]{:S(2)}, u32[]{:S(2)}) collective-permute-start(f32[38,6,1,128]{3,0,2,1:T(8,128)S(1)} %copy.290), channel_id=1, source_target_pairs={{2,0},{4,2},{6,4},{0,6},{3,1},{5,3},{7,5},{1,7},{10,8},{12,10},{14... | collective-permute-start | bytes 350216 | tf_op jit(solution)/shard_map/ppermute | solution.py:42
  81.3 2.6 %collective-permute-done.8 = f32[38,6,1,128]{3,0,2,1:T(8,128)S(1)} collective-permute-done((f32[38,6,1,128]{3,0,2,1:T(8,128)S(1)}, f32[38,6,1,128]{3,0,2,1:T(8,128)S(1)}, u32[]{:S(2)}, u32[]{:S(2)}) %collective-permute-start.8) | collective-permute-done | bytes 116768 | tf_op jit(solution)/shard_map/ppermute | solution.py:40
  83.8 0.1 copy.289
  84.0 1.9 %collective-permute-done.9 = f32[38,6,1,128]{3,0,2,1:T(8,128)S(1)} collective-permute-done((f32[38,6,1,128]{3,0,2,1:T(8,128)S(1)}, f32[38,6,1,128]{3,0,2,1:T(8,128)S(1)}, u32[]{:S(2)}, u32[]{:S(2)}) %collective-permute-start.9) | collective-permute-done | bytes 116768 | tf_op jit(solution)/shard_map/ppermute | solution.py:42
  85.9 0.1 copy.291
  86.0 0.5 pad_maximum_fusion
  86.5 3.2 %fusion.105 = (f32[38,6,18,1]{3,2,1,0:T(8,128)}, f32[38,6,18,1]{3,2,1,0:T(8,128)}) fusion(f32[38,6,18,128]{3,2,1,0:T(8,128)S(1)} %pad_maximum_fusion), kind=kLoop, calls=%fused_computation.399 | loop fusion | bytes 65664 | tf_op jit(solution)/shard_map/slice | solution.py:36
  89.7 3.0 %copy.294 = f32[38,6,18,1]{0,2,3,1:T(8,128)S(1)} copy(f32[38,6,18,1]{3,2,1,0:T(8,128)} %get-tuple-element.53) | data formatting | bytes 32832 | tf_op jit(solution)/shard_map/slice | solution.py:37
  92.8 4.6 %collective-permute-start.10 = (f32[38,6,18,1]{0,2,3,1:T(8,128)S(1)}, f32[38,6,18,1]{0,2,3,1:T(8,128)S(1)}, u32[]{:S(2)}, u32[]{:S(2)}) collective-permute-start(f32[38,6,18,1]{0,2,3,1:T(8,128)S(1)} %copy.294), channel_id=1, source_target_pairs={{0,1},{1,0},{2,3},{3,2},{4,5},{5,4},{6,7},{7,6},{8,9},{9,8},{10,11... | collective-permute-start | bytes 49256 | tf_op jit(solution)/shard_map/ppermute | solution.py:40
  97.4 3.0 %copy.296 = f32[38,6,18,1]{0,2,3,1:T(8,128)S(1)} copy(f32[38,6,18,1]{3,2,1,0:T(8,128)} %get-tuple-element.52) | data formatting | bytes 32832 | tf_op jit(solution)/shard_map/slice | solution.py:36
  100.4 1.5 %collective-permute-start.11 = (f32[38,6,18,1]{0,2,3,1:T(8,128)S(1)}, f32[38,6,18,1]{0,2,3,1:T(8,128)S(1)}, u32[]{:S(2)}, u32[]{:S(2)}) collective-permute-start(f32[38,6,18,1]{0,2,3,1:T(8,128)S(1)} %copy.296), channel_id=1, source_target_pairs={{1,0},{0,1},{3,2},{2,3},{5,4},{4,5},{7,6},{6,7},{9,8},{8,9},{11,10... | collective-permute-start | bytes 49256 | tf_op jit(solution)/shard_map/ppermute | solution.py:42
  101.9 2.8 %copy.295 = f32[38,6,18,1]{3,2,1,0:T(8,128)} copy(f32[38,6,18,1]{0,2,3,1:T(8,128)S(1)} %collective-permute-done.10) | data formatting | bytes 32832 | tf_op jit(solution)/shard_map/ppermute | solution.py:40
  104.7 0.9 constant_dynamic-update-slice_fusion.91
  105.5 3.2 %collective-permute-done.11 = f32[38,6,18,1]{0,2,3,1:T(8,128)S(1)} collective-permute-done((f32[38,6,18,1]{0,2,3,1:T(8,128)S(1)}, f32[38,6,18,1]{0,2,3,1:T(8,128)S(1)}, u32[]{:S(2)}, u32[]{:S(2)}) %collective-permute-start.11) | collective-permute-done | bytes 16448 | tf_op jit(solution)/shard_map/ppermute | solution.py:42
  108.7 2.8 %copy.297 = f32[38,6,18,1]{3,2,1,0:T(8,128)} copy(f32[38,6,18,1]{0,2,3,1:T(8,128)S(1)} %collective-permute-done.11) | data formatting | bytes 32832 | tf_op jit(solution)/shard_map/ppermute | solution.py:42
  111.5 0.9 constant_dynamic-update-slice_fusion.90
  112.5 1.7 %copy-done.1 = f32[38,6,18,1]{3,2,1,0:T(8,128)S(1)} copy-done((f32[38,6,18,1]{3,2,1,0:T(8,128)S(1)}, f32[38,6,18,1]{3,2,1,0:T(8,128)}, u32[]{:S(2)}) %copy-start.1) | copy-done | bytes 16440
  114.3 1.7 %copy-done = f32[38,6,18,1]{3,2,1,0:T(8,128)S(1)} copy-done((f32[38,6,18,1]{3,2,1,0:T(8,128)S(1)}, f32[38,6,18,1]{3,2,1,0:T(8,128)}, u32[]{:S(2)}) %copy-start) | copy-done | bytes 16440
  116.2 0.1 constant_dynamic-update-slice_fusion.81
  116.3 1.0 copy-done.5
  117.4 0.1 constant_dynamic-update-slice_fusion.79
  117.6 0.1 constant_dynamic-update-slice_fusion.71
  117.7 0.1 constant_dynamic-update-slice_fusion.78
  117.8 0.1 constant_dynamic-update-slice_fusion.67
  118.0 0.1 constant_dynamic-update-slice_fusion.77
  118.2 0.7 copy-done.4
  119.1 0.1 constant_dynamic-update-slice_fusion.60
  119.2 0.1 constant_dynamic-update-slice_fusion.59
  119.4 0.8 copy-done.6
  (113 shorter events, 2.6 us)
Async XLA Ops:
  0.6 44.2 %copy-start.3 = (f32[19,4,16,128]{3,2,1,0:T(8,128)S(1)}, f32[19,4,16,128]{3,2,1,0:T(8,128)}, u32[]{:S(2)}) copy-start(f32[19,4,16,128]{3,2,1,0:T(8,128)} %param.4) | copy-start | bytes 1867780
  0.6 44.0 %copy-start.2 = (f32[19,4,16,128]{3,2,1,0:T(8,128)S(1)}, f32[19,4,16,128]{3,2,1,0:T(8,128)}, u32[]{:S(2)}) copy-start(f32[19,4,16,128]{3,2,1,0:T(8,128)} %param.3) | copy-start | bytes 1867780
  1.9 11.4 %collective-permute-start.3 = (f32[4,1,128]{2,1,0:T(1,128)S(1)}, f32[4,1,128]{2,1,0:T(1,128)S(1)}, u32[]{:S(2)}, u32[]{:S(2)}) collective-permute-start(f32[4,1,128]{2,1,0:T(1,128)S(1)} %get-tuple-element.108), channel_id=1, source_target_pairs={{2,0},{4,2},{6,4},{0,6},{3,1},{5,3},{7,5},{1,7},{10,8},{12,10},{14... | collective-permute-start | bytes 6152 | tf_op jit(solution)/shard_map/ppermute | solution.py:42
  2.8 10.5 %collective-permute-start.2 = (f32[4,1,128]{2,1,0:T(1,128)S(1)}, f32[4,1,128]{2,1,0:T(1,128)S(1)}, u32[]{:S(2)}, u32[]{:S(2)}) collective-permute-start(f32[4,1,128]{2,1,0:T(1,128)S(1)} %get-tuple-element.109), channel_id=1, source_target_pairs={{0,2},{2,4},{4,6},{6,0},{1,3},{3,5},{5,7},{7,1},{8,10},{10,12},{12... | collective-permute-start | bytes 6152 | tf_op jit(solution)/shard_map/ppermute | solution.py:40
  5.2 26.1 %collective-permute-start.1 = (f32[1,1,16,128]{3,2,1,0:T(8,128)S(1)}, f32[1,1,16,128]{3,2,1,0:T(8,128)S(1)}, u32[]{:S(2)}, u32[]{:S(2)}) collective-permute-start(f32[1,1,16,128]{3,2,1,0:T(8,128)S(1)} %get-tuple-element.114), channel_id=1, source_target_pairs={{8,0},{16,8},{24,16},{32,24},{40,32},{48,40},{56,48},{64,56},{72,6... | collective-permute-start | bytes 24584 | tf_op jit(solution)/shard_map/ppermute | solution.py:42
  11.2 8.1 %collective-permute-start = (f32[1,1,16,128]{3,2,1,0:T(8,128)S(1)}, f32[1,1,16,128]{3,2,1,0:T(8,128)S(1)}, u32[]{:S(2)}, u32[]{:S(2)}) collective-permute-start(f32[1,1,16,128]{3,2,1,0:T(8,128)S(1)} %get-tuple-element.115), channel_id=1, source_target_pairs={{0,8},{8,16},{16,24},{24,32},{32,40},{40,48},{48,56},{56,64},{64,7... | collective-permute-start | bytes 24584 | tf_op jit(solution)/shard_map/ppermute | solution.py:40
  13.4 29.9 %collective-permute-start.5 = (f32[4,18,1]{2,1,0:T(8,128)S(1)}, f32[4,18,1]{2,1,0:T(8,128)S(1)}, u32[]{:S(2)}, u32[]{:S(2)}) collective-permute-start(f32[4,18,1]{2,1,0:T(8,128)S(1)} %get-tuple-element.106), channel_id=1, source_target_pairs={{1,0},{0,1},{3,2},{2,3},{5,4},{4,5},{7,6},{6,7},{9,8},{8,9},{11,10... | collective-permute-start | bytes 872 | tf_op jit(solution)/shard_map/ppermute | solution.py:42
  17.9 25.3 %collective-permute-start.4 = (f32[4,18,1]{2,1,0:T(8,128)S(1)}, f32[4,18,1]{2,1,0:T(8,128)S(1)}, u32[]{:S(2)}, u32[]{:S(2)}) collective-permute-start(f32[4,18,1]{2,1,0:T(8,128)S(1)} %get-tuple-element.107), channel_id=1, source_target_pairs={{0,1},{1,0},{2,3},{3,2},{4,5},{5,4},{6,7},{7,6},{8,9},{9,8},{10,11... | collective-permute-start | bytes 872 | tf_op jit(solution)/shard_map/ppermute | solution.py:40
  45.4 20.5 %collective-permute-start.7 = (f32[10,1,16,128]{3,2,1,0:T(8,128)S(1)}, f32[10,1,16,128]{3,2,1,0:T(8,128)S(1)}, u32[]{:S(2)}, u32[]{:S(2)}) collective-permute-start(f32[10,1,16,128]{3,2,1,0:T(8,128)S(1)} %get-tuple-element.92), channel_id=1, source_target_pairs={{8,0},{16,8},{24,16},{32,24},{40,32},{48,40},{56,48},{64,56},{72,6... | collective-permute-start | bytes 245768 | tf_op jit(solution)/shard_map/ppermute | solution.py:42
  45.5 7.9 %collective-permute-start.6 = (f32[10,1,16,128]{3,2,1,0:T(8,128)S(1)}, f32[10,1,16,128]{3,2,1,0:T(8,128)S(1)}, u32[]{:S(2)}, u32[]{:S(2)}) collective-permute-start(f32[10,1,16,128]{3,2,1,0:T(8,128)S(1)} %get-tuple-element.93), channel_id=1, source_target_pairs={{0,8},{8,16},{16,24},{24,32},{32,40},{40,48},{48,56},{56,64},{64,7... | collective-permute-start | bytes 245768 | tf_op jit(solution)/shard_map/ppermute | solution.py:40
  78.9 5.0 %collective-permute-start.8 = (f32[38,6,1,128]{3,0,2,1:T(8,128)S(1)}, f32[38,6,1,128]{3,0,2,1:T(8,128)S(1)}, u32[]{:S(2)}, u32[]{:S(2)}) collective-permute-start(f32[38,6,1,128]{3,0,2,1:T(8,128)S(1)} %copy.288), channel_id=1, source_target_pairs={{0,2},{2,4},{4,6},{6,0},{1,3},{3,5},{5,7},{7,1},{8,10},{10,12},{12... | collective-permute-start | bytes 350216 | tf_op jit(solution)/shard_map/ppermute | solution.py:40
  79.6 6.3 %collective-permute-start.9 = (f32[38,6,1,128]{3,0,2,1:T(8,128)S(1)}, f32[38,6,1,128]{3,0,2,1:T(8,128)S(1)}, u32[]{:S(2)}, u32[]{:S(2)}) collective-permute-start(f32[38,6,1,128]{3,0,2,1:T(8,128)S(1)} %copy.290), channel_id=1, source_target_pairs={{2,0},{4,2},{6,4},{0,6},{3,1},{5,3},{7,5},{1,7},{10,8},{12,10},{14... | collective-permute-start | bytes 350216 | tf_op jit(solution)/shard_map/ppermute | solution.py:42
  92.8 9.1 %collective-permute-start.10 = (f32[38,6,18,1]{0,2,3,1:T(8,128)S(1)}, f32[38,6,18,1]{0,2,3,1:T(8,128)S(1)}, u32[]{:S(2)}, u32[]{:S(2)}) collective-permute-start(f32[38,6,18,1]{0,2,3,1:T(8,128)S(1)} %copy.294), channel_id=1, source_target_pairs={{0,1},{1,0},{2,3},{3,2},{4,5},{5,4},{6,7},{7,6},{8,9},{9,8},{10,11... | collective-permute-start | bytes 49256 | tf_op jit(solution)/shard_map/ppermute | solution.py:40
  100.4 8.3 %collective-permute-start.11 = (f32[38,6,18,1]{0,2,3,1:T(8,128)S(1)}, f32[38,6,18,1]{0,2,3,1:T(8,128)S(1)}, u32[]{:S(2)}, u32[]{:S(2)}) collective-permute-start(f32[38,6,18,1]{0,2,3,1:T(8,128)S(1)} %copy.296), channel_id=1, source_target_pairs={{1,0},{0,1},{3,2},{2,3},{5,4},{4,5},{7,6},{6,7},{9,8},{8,9},{11,10... | collective-permute-start | bytes 49256 | tf_op jit(solution)/shard_map/ppermute | solution.py:42
  112.4 1.8 %copy-start.1 = (f32[38,6,18,1]{3,2,1,0:T(8,128)S(1)}, f32[38,6,18,1]{3,2,1,0:T(8,128)}, u32[]{:S(2)}) copy-start(f32[38,6,18,1]{3,2,1,0:T(8,128)} %copy.297) | copy-start | bytes 49252
  114.2 1.8 %copy-start = (f32[38,6,18,1]{3,2,1,0:T(8,128)S(1)}, f32[38,6,18,1]{3,2,1,0:T(8,128)}, u32[]{:S(2)}) copy-start(f32[38,6,18,1]{3,2,1,0:T(8,128)} %copy.295) | copy-start | bytes 49252
  116.2 1.1 copy-start.5
  118.1 0.8 copy-start.4
  119.4 0.8 copy-start.6
where the time goes:
time: 121 us; the launch traced here: 120 us
  blocking collectives  48.6 us (40%)
  starting transfers between devices  24.3 us (20%)
  local copies, waits for them, and re-layouts  22.6 us (19%)
  waiting for transfers between devices  13.7 us (11%)
  other arithmetic  8.9 us (7%)
  between operations  2.11 us (2%)
    all_gather x2, blocking collectives, sliding(): lax.all_gather(above, 'gy', axis=1, tiled=True)  24.3 us
    all_gather x2, blocking collectives, sliding(): lax.all_gather(below, 'gy', axis=1, tiled=True)  24.3 us
    ppermute x6, starting transfers between devices, with_halo(): lax.ppermute(head, axis, [((i + 1) % count, i) for i in range(count)])  14.7 us
    ppermute x6, starting transfers between devices, with_halo(): lax.ppermute(tail, axis, [(i, (i + 1) % count) for i in range(count)])  9.57 us
    ppermute x6, waiting for transfers between devices, with_halo(): lax.ppermute(tail, axis, [(i, (i + 1) % count) for i in range(count)])  8.57 us
    unnamed x27, local copies, waits for them, and re-layouts  6.9 us
    slice x7, local copies, waits for them, and re-layouts, with_halo(): head = lax.slice_in_dim(cells, 0, width, axis=dim)  6.39 us
    ppermute x6, waiting for transfers between devices, with_halo(): lax.ppermute(head, axis, [((i + 1) % count, i) for i in range(count)])  5.11 us
  transfers between devices with their start and end apart: 12, of which 4 were waited for; matrix products, arithmetic and copies ran while one was open for 8% of the time, Pallas kernels for 0%

commit v1 on v0

--- a/solution.py
+++ b/solution.py
@@ -28,6 +28,24 @@
 STIFFNESS = 0.5
 TAU_FLUID = 0.8
 TAU_ORDER = 0.9
+
+
+def collect(array, axis, dim):
+    ways, here, step = (lax.axis_size(axis), lax.axis_index(axis), array.shape[dim])
+    dims = [n * ways if d == dim else n for d, n in enumerate(array.shape)]
+    full = lax.dynamic_update_slice_in_dim(
+        jnp.zeros(dims, array.dtype), array, here * step, axis=dim
+    )
+    going_up = going_down = array
+    for far in range(1, ways // 2 + 1):
+        going_up = lax.ppermute(going_up, axis, [(d, (d + 1) % ways) for d in range(ways)])
+        full = lax.dynamic_update_slice_in_dim(full, going_up, (here - far) % ways * step, axis=dim)
+        if 2 * far < ways:
+            going_down = lax.ppermute(going_down, axis, [(d, (d - 1) % ways) for d in range(ways)])
+            full = lax.dynamic_update_slice_in_dim(
+                full, going_down, (here + far) % ways * step, axis=dim
+            )
+    return full
 
 
 def with_halo(cells, sides, width):
@@ -115,7 +133,7 @@
     below = extended[:, 0]
     above = extended[:, 3]
     whole_below, whole_above = (
-        lax.all_gather(below, "gy", axis=1, tiled=True),
+        collect(below, "gy", 1),
         lax.all_gather(above, "gy", axis=1, tiled=True),
     )
     rows = below.shape[1]

time: 121 us -> 114 us (0.942)
  blocking collectives: 48.6 us -> 24.9 us
  starting transfers between devices: 24.3 us -> 35 us
  waiting for transfers between devices: 13.7 us -> 19.7 us
    all_gather x2 -> x0, blocking collectives: 24.3 us -> none  [sliding(): lax.all_gather(below, 'gy', axis=1, tiled=True)]
    ppermute x0 -> x6, starting transfers between devices: none -> 9.28 us  [the longest x4 7.55 us: collect(): lax.ppermute(going_up, axis, [(d, (d + 1) % ways) for d in range(ways)])]
    ppermute x0 -> x6, waiting for transfers between devices: none -> 4.14 us  [the longest x4 4.14 us: collect(): lax.ppermute(going_up, axis, [(d, (d + 1) % ways) for d in range(ways)])]
    ppermute x6, starting transfers between devices: 9.57 us -> 12.1 us  [with_halo(): lax.ppermute(tail, axis, [(i, (i + 1) % count) for i in range(count)])]
    ppermute x6, waiting for transfers between devices: 5.11 us -> 6.72 us  [with_halo(): lax.ppermute(head, axis, [((i + 1) % count, i) for i in range(count)])]
    unnamed x27 -> x25, local copies, waits for them, and re-layouts: 6.9 us -> 7.14 us
    ppermute x3 -> x2, local copies, waits for them, and re-layouts: 2.97 us -> 2.8 us  [with_halo(): lax.ppermute(tail, axis, [(i, (i + 1) % count) for i in range(count)])]
    unnamed x56 -> x60, other arithmetic: 3.92 us -> 3.97 us
  transfers between devices with their start and end apart: 12 -> 18, of which waited for: 4 -> 7; matrix products, arithmetic and copies ran while one was open for 8% -> 8% of each run, Pallas kernels for 0% -> 0%
where the time goes in v1:
time: 114 us; the launch traced here: 113 us
  starting transfers between devices  35 us (31%)
  blocking collectives  24.9 us (22%)
  local copies, waits for them, and re-layouts  22.3 us (20%)
  waiting for transfers between devices  19.7 us (17%)
  other arithmetic  8.93 us (8%)
  between operations  2.19 us (2%)
    all_gather x2, blocking collectives, sliding(): lax.all_gather(above, 'gy', axis=1, tiled=True)  24.9 us
    ppermute x6, starting transfers between devices, with_halo(): lax.ppermute(head, axis, [((i + 1) % count, i) for i in range(count)])  13.6 us
    ppermute x6, starting transfers between devices, with_halo(): lax.ppermute(tail, axis, [(i, (i + 1) % count) for i in range(count)])  12.1 us
    ppermute x6, waiting for transfers between devices, with_halo(): lax.ppermute(tail, axis, [(i, (i + 1) % count) for i in range(count)])  8.84 us
    ppermute x4, starting transfers between devices, collect(): lax.ppermute(going_up, axis, [(d, (d + 1) % ways) for d in range(ways)])  7.55 us
    unnamed x25, local copies, waits for them, and re-layouts  7.14 us
    ppermute x6, waiting for transfers between devices, with_halo(): lax.ppermute(head, axis, [((i + 1) % count, i) for i in range(count)])  6.72 us
    slice x7, local copies, waits for them, and re-layouts, with_halo(): head = lax.slice_in_dim(cells, 0, width, axis=dim)  6.23 us
  transfers between devices with their start and end apart: 18, of which 7 were waited for; matrix products, arithmetic and copies ran while one was open for 8% of the time, Pallas kernels for 0%

profile of v1, /device:TPU:6, one launch (start us, length us, event | category | flops | bytes accessed | tf_op | source)
XLA Modules:
  0.0 113.0 jit_solution(1753185039659289932)
XLA Ops:
  0.7 1.2 %reduce_sum.19 = f32[4,16,128]{2,1,0:T(8,128)S(1)} reduce(f32[19,4,16,128]{3,2,1,0:T(8,128)} %param.4, f32[]{:T(128)} %constant.123.clone.1), dimensions={0}, to_apply=%region_1.2 | reduce | flops 147456 | bytes 655364 | tf_op jit(solution)/shard_map/reduce_sum | solution.py:172
  1.9 0.9 collective-permute-start.6
  2.8 2.4 %collective-permute-start.5 = (f32[4,1,128]{2,1,0:T(1,128)S(1)}, f32[4,1,128]{2,1,0:T(1,128)S(1)}, u32[]{:S(2)}, u32[]{:S(2)}) collective-permute-start(f32[4,1,128]{2,1,0:T(1,128)S(1)} %get-tuple-element.99), channel_id=1, source_target_pairs={{0,2},{2,4},{4,6},{6,0},{1,3},{3,5},{5,7},{7,1},{8,10},{10,12},{12... | collective-permute-start | bytes 6152 | tf_op jit(solution)/shard_map/ppermute | solution.py:58
  5.2 6.0 %collective-permute-start.4 = (f32[1,1,16,128]{3,2,1,0:T(8,128)S(1)}, f32[1,1,16,128]{3,2,1,0:T(8,128)S(1)}, u32[]{:S(2)}, u32[]{:S(2)}) collective-permute-start(f32[1,1,16,128]{3,2,1,0:T(8,128)S(1)} %get-tuple-element.104), channel_id=1, source_target_pairs={{8,0},{16,8},{24,16},{32,24},{40,32},{48,40},{56,48},{64,56},{72,6... | collective-permute-start | bytes 24584 | tf_op jit(solution)/shard_map/ppermute | solution.py:60
  12.1 1.1 reduce_sum.18
  13.4 4.5 %collective-permute-start.8 = (f32[4,18,1]{2,1,0:T(8,128)S(1)}, f32[4,18,1]{2,1,0:T(8,128)S(1)}, u32[]{:S(2)}, u32[]{:S(2)}) collective-permute-start(f32[4,18,1]{2,1,0:T(8,128)S(1)} %get-tuple-element.96), channel_id=1, source_target_pairs={{1,0},{0,1},{3,2},{2,3},{5,4},{4,5},{7,6},{6,7},{9,8},{8,9},{11,10... | collective-permute-start | bytes 872 | tf_op jit(solution)/shard_map/ppermute | solution.py:60
  17.9 1.4 %collective-permute-start.7 = (f32[4,18,1]{2,1,0:T(8,128)S(1)}, f32[4,18,1]{2,1,0:T(8,128)S(1)}, u32[]{:S(2)}, u32[]{:S(2)}) collective-permute-start(f32[4,18,1]{2,1,0:T(8,128)S(1)} %get-tuple-element.97), channel_id=1, source_target_pairs={{0,1},{1,0},{2,3},{3,2},{4,5},{5,4},{6,7},{7,6},{8,9},{9,8},{10,11... | collective-permute-start | bytes 872 | tf_op jit(solution)/shard_map/ppermute | solution.py:58
  19.4 0.3 collective-permute-start.1
  19.7 1.7 %collective-permute-start.2 = (f32[1,16,128]{2,1,0:T(8,128)S(1)}, f32[1,16,128]{2,1,0:T(8,128)S(1)}, u32[]{:S(2)}, u32[]{:S(2)}) collective-permute-start(f32[1,16,128]{2,1,0:T(8,128)S(1)} %bitcast.732), channel_id=1, source_target_pairs={{0,6},{2,0},{4,2},{6,4},{1,7},{3,1},{5,3},{7,5},{8,14},{10,8},{12,... | collective-permute-start | bytes 24584 | tf_op jit(solution)/shard_map/ppermute | solution.py:44
  21.4 11.9 %all-gather = f32[1,1,64,128]{3,2,1,0:T(8,128)S(1)} all-gather(f32[1,1,16,128]{3,2,1,0:T(8,128)S(1)} %collective-permute-done.4), channel_id=2, replica_groups=mesh['gx'=32,'gy'=4,'gz'=2] {'gy'}, dimensions={2}, use_global_device_ids=true | all-gather | bytes 40960 | tf_op jit(solution)/shard_map/all_gather | solution.py:137
  33.4 1.6 %collective-permute-start.3 = (f32[1,16,128]{2,1,0:T(8,128)S(1)}, f32[1,16,128]{2,1,0:T(8,128)S(1)}, u32[]{:S(2)}, u32[]{:S(2)}) collective-permute-start(f32[1,16,128]{2,1,0:T(8,128)S(1)} %collective-permute-done.1), channel_id=1, source_target_pairs={{0,2},{2,4},{4,6},{6,0},{1,3},{3,5},{5,7},{7,1},{8,10},{10,12},{12... | collective-permute-start | bytes 24584 | tf_op jit(solution)/shard_map/ppermute | solution.py:41
  35.0 2.1 %collective-permute-done.3 = f32[1,16,128]{2,1,0:T(8,128)S(1)} collective-permute-done((f32[1,16,128]{2,1,0:T(8,128)S(1)}, f32[1,16,128]{2,1,0:T(8,128)S(1)}, u32[]{:S(2)}, u32[]{:S(2)}) %collective-permute-start.3) | collective-permute-done | bytes 8224 | tf_op jit(solution)/shard_map/ppermute | solution.py:41
  37.1 1.4 %bitcast_subtract_fusion.16 = (f32[4,16,128]{2,1,0:T(8,128)S(1)}, f32[4,16,128]{2,1,0:T(8,128)S(1)}, f32[4,16,128]{2,1,0:T(8,128)S(1)}, f32[4,16,128]{2,1,0:T(8,...) fusion(f32[4,16,128]{2,1,0:T(8,128)S(1)} %reduce_sum.19, ...), kind=kLoop, calls=%fused_computation.191 | loop fusion | flops 2064384 | bytes 1512000 | tf_op jit(solution)/shard_map/sub | solution.py:121
  39.3 0.6 collective-permute-start.13
  39.9 0.8 copy.315
  41.3 6.4 %collective-permute-done.9 = f32[10,1,16,128]{3,2,0,1:T(8,128)S(1)} collective-permute-done((f32[10,1,16,128]{3,2,0,1:T(8,128)S(1)}, f32[10,1,16,128]{3,2,0,1:T(8,128)S(1)}, u32[]{:S(2)}, u32[]{:S(2)}) %collective-permute-start.9) | collective-permute-done | bytes 81952 | tf_op jit(solution)/shard_map/ppermute | solution.py:58
  47.6 2.7 %collective-permute-start.10 = (f32[10,16,128]{2,1,0:T(8,128)S(1)}, f32[10,16,128]{2,1,0:T(8,128)S(1)}, u32[]{:S(2)}, u32[]{:S(2)}) collective-permute-start(f32[10,16,128]{2,1,0:T(8,128)S(1)} %bitcast.729), channel_id=1, source_target_pairs={{0,2},{2,4},{4,6},{6,0},{1,3},{3,5},{5,7},{7,1},{8,10},{10,12},{12... | collective-permute-start | bytes 245768 | tf_op jit(solution)/shard_map/ppermute | solution.py:41
  50.5 13.0 %all-gather.1 = f32[10,1,64,128]{3,1,0,2:T(1,128)S(1)} all-gather(f32[10,1,16,128]{3,1,0,2:T(1,128)S(1)} %copy.202), channel_id=3, replica_groups=mesh['gx'=32,'gy'=4,'gz'=2] {'gy'}, dimensions={2}, use_global_device_ids=true | all-gather | bytes 409600 | tf_op jit(solution)/shard_map/all_gather | solution.py:137
  63.5 0.1 maximum_bitcast_fusion.1
  63.7 2.9 %collective-permute-start.12 = (f32[10,16,128]{2,1,0:T(8,128)S(1)}, f32[10,16,128]{2,1,0:T(8,128)S(1)}, u32[]{:S(2)}, u32[]{:S(2)}) collective-permute-start(f32[10,16,128]{2,1,0:T(8,128)S(1)} %collective-permute-done.10), channel_id=1, source_target_pairs={{0,2},{2,4},{4,6},{6,0},{1,3},{3,5},{5,7},{7,1},{8,10},{10,12},{12... | collective-permute-start | bytes 245768 | tf_op jit(solution)/shard_map/ppermute | solution.py:41
  66.6 2.0 %collective-permute-done.12 = f32[10,16,128]{2,1,0:T(8,128)S(1)} collective-permute-done((f32[10,16,128]{2,1,0:T(8,128)S(1)}, f32[10,16,128]{2,1,0:T(8,128)S(1)}, u32[]{:S(2)}, u32[]{:S(2)}) %collective-permute-start.12) | collective-permute-done | bytes 81952 | tf_op jit(solution)/shard_map/ppermute | solution.py:41
  68.7 0.1 maximum_bitcast_fusion.2
  68.8 0.2 fusion
  69.0 3.7 %collective-permute-start.14 = (f32[38,6,1,128]{3,0,2,1:T(8,128)S(1)}, f32[38,6,1,128]{3,0,2,1:T(8,128)S(1)}, u32[]{:S(2)}, u32[]{:S(2)}) collective-permute-start(f32[38,6,1,128]{3,0,2,1:T(8,128)S(1)} %copy.222), channel_id=1, source_target_pairs={{0,2},{2,4},{4,6},{6,0},{1,3},{3,5},{5,7},{7,1},{8,10},{10,12},{12... | collective-permute-start | bytes 350216 | tf_op jit(solution)/shard_map/ppermute | solution.py:58
  72.8 2.3 %collective-permute-done.14 = f32[38,6,1,128]{3,0,2,1:T(8,128)S(1)} collective-permute-done((f32[38,6,1,128]{3,0,2,1:T(8,128)S(1)}, f32[38,6,1,128]{3,0,2,1:T(8,128)S(1)}, u32[]{:S(2)}, u32[]{:S(2)}) %collective-permute-start.14) | collective-permute-done | bytes 116768 | tf_op jit(solution)/shard_map/ppermute | solution.py:58
  75.2 0.1 copy.223
  75.3 3.6 %collective-permute-done.15 = f32[38,6,1,128]{3,0,2,1:T(8,128)S(1)} collective-permute-done((f32[38,6,1,128]{3,0,2,1:T(8,128)S(1)}, f32[38,6,1,128]{3,0,2,1:T(8,128)S(1)}, u32[]{:S(2)}, u32[]{:S(2)}) %collective-permute-start.15) | collective-permute-done | bytes 116768 | tf_op jit(solution)/shard_map/ppermute | solution.py:60
  78.9 0.1 copy.225
  79.0 0.4 pad_maximum_fusion
  79.5 3.2 %fusion.105 = (f32[38,6,18,1]{3,2,0,1:T(8,128)}, f32[38,6,18,1]{3,2,0,1:T(8,128)}) fusion(f32[38,6,18,128]{3,2,0,1:T(8,128)S(1)} %pad_maximum_fusion), kind=kLoop, calls=%fused_computation.408 | loop fusion | bytes 65664 | tf_op jit(solution)/shard_map/slice | solution.py:54
  82.7 2.9 %copy.228 = f32[38,6,18,1]{0,2,3,1:T(8,128)S(1)} copy(f32[38,6,18,1]{3,2,0,1:T(8,128)} %get-tuple-element.53) | data formatting | bytes 32832 | tf_op jit(solution)/shard_map/slice | solution.py:55
  85.6 4.6 %collective-permute-start.16 = (f32[38,6,18,1]{0,2,3,1:T(8,128)S(1)}, f32[38,6,18,1]{0,2,3,1:T(8,128)S(1)}, u32[]{:S(2)}, u32[]{:S(2)}) collective-permute-start(f32[38,6,18,1]{0,2,3,1:T(8,128)S(1)} %copy.228), channel_id=1, source_target_pairs={{0,1},{1,0},{2,3},{3,2},{4,5},{5,4},{6,7},{7,6},{8,9},{9,8},{10,11... | collective-permute-start | bytes 49256 | tf_op jit(solution)/shard_map/ppermute | solution.py:58
  90.2 2.9 %copy.230 = f32[38,6,18,1]{0,2,3,1:T(8,128)S(1)} copy(f32[38,6,18,1]{3,2,0,1:T(8,128)} %get-tuple-element.52) | data formatting | bytes 32832 | tf_op jit(solution)/shard_map/slice | solution.py:54
  93.1 1.5 %collective-permute-start.17 = (f32[38,6,18,1]{0,2,3,1:T(8,128)S(1)}, f32[38,6,18,1]{0,2,3,1:T(8,128)S(1)}, u32[]{:S(2)}, u32[]{:S(2)}) collective-permute-start(f32[38,6,18,1]{0,2,3,1:T(8,128)S(1)} %copy.230), channel_id=1, source_target_pairs={{1,0},{0,1},{3,2},{2,3},{5,4},{4,5},{7,6},{6,7},{9,8},{8,9},{11,10... | collective-permute-start | bytes 49256 | tf_op jit(solution)/shard_map/ppermute | solution.py:60
  94.6 0.1 collective-permute-done.16
  94.7 2.7 %copy.229 = f32[38,6,18,1]{3,2,0,1:T(8,128)} copy(f32[38,6,18,1]{0,2,3,1:T(8,128)S(1)} %collective-permute-done.16) | data formatting | bytes 32832 | tf_op jit(solution)/shard_map/ppermute | solution.py:58
  97.4 0.9 constant_dynamic-update-slice_fusion.91
  98.3 3.1 %collective-permute-done.17 = f32[38,6,18,1]{0,2,3,1:T(8,128)S(1)} collective-permute-done((f32[38,6,18,1]{0,2,3,1:T(8,128)S(1)}, f32[38,6,18,1]{0,2,3,1:T(8,128)S(1)}, u32[]{:S(2)}, u32[]{:S(2)}) %collective-permute-start.17) | collective-permute-done | bytes 16448 | tf_op jit(solution)/shard_map/ppermute | solution.py:60
  101.4 2.7 %copy.231 = f32[38,6,18,1]{3,2,0,1:T(8,128)} copy(f32[38,6,18,1]{0,2,3,1:T(8,128)S(1)} %collective-permute-done.17) | data formatting | bytes 32832 | tf_op jit(solution)/shard_map/ppermute | solution.py:60
  104.1 0.9 constant_dynamic-update-slice_fusion.90
  105.1 1.7 %copy-done.1 = f32[38,6,18,1]{3,2,0,1:T(8,128)S(1)} copy-done((f32[38,6,18,1]{3,2,0,1:T(8,128)S(1)}, f32[38,6,18,1]{3,2,0,1:T(8,128)}, u32[]{:S(2)}) %copy-start.1) | copy-done | bytes 16440
  106.9 1.7 %copy-done = f32[38,6,18,1]{3,2,0,1:T(8,128)S(1)} copy-done((f32[38,6,18,1]{3,2,0,1:T(8,128)S(1)}, f32[38,6,18,1]{3,2,0,1:T(8,128)}, u32[]{:S(2)}) %copy-start) | copy-done | bytes 16440
  108.9 1.0 copy-done.4
  109.9 0.1 constant_dynamic-update-slice_fusion.79
  110.3 0.1 constant_dynamic-update-slice_fusion.78
  110.7 0.9 copy.235
  111.8 0.1 constant_dynamic-update-slice_fusion.60
  112.1 0.9 copy.234
  (133 shorter events, 3.1 us)
Async XLA Ops:
  0.6 37.9 %copy-start.3 = (f32[19,4,16,128]{3,2,1,0:T(8,128)S(1)}, f32[19,4,16,128]{3,2,1,0:T(8,128)}, u32[]{:S(2)}) copy-start(f32[19,4,16,128]{3,2,1,0:T(8,128)} %param.4) | copy-start | bytes 1867780
  0.6 37.9 %copy-start.2 = (f32[19,4,16,128]{3,2,1,0:T(8,128)S(1)}, f32[19,4,16,128]{3,2,1,0:T(8,128)}, u32[]{:S(2)}) copy-start(f32[19,4,16,128]{3,2,1,0:T(8,128)} %param.3) | copy-start | bytes 1867780
  1.9 11.4 %collective-permute-start.6 = (f32[4,1,128]{2,1,0:T(1,128)S(1)}, f32[4,1,128]{2,1,0:T(1,128)S(1)}, u32[]{:S(2)}, u32[]{:S(2)}) collective-permute-start(f32[4,1,128]{2,1,0:T(1,128)S(1)} %get-tuple-element.98), channel_id=1, source_target_pairs={{2,0},{4,2},{6,4},{0,6},{3,1},{5,3},{7,5},{1,7},{10,8},{12,10},{14... | collective-permute-start | bytes 6152 | tf_op jit(solution)/shard_map/ppermute | solution.py:60
  2.8 10.5 %collective-permute-start.5 = (f32[4,1,128]{2,1,0:T(1,128)S(1)}, f32[4,1,128]{2,1,0:T(1,128)S(1)}, u32[]{:S(2)}, u32[]{:S(2)}) collective-permute-start(f32[4,1,128]{2,1,0:T(1,128)S(1)} %get-tuple-element.99), channel_id=1, source_target_pairs={{0,2},{2,4},{4,6},{6,0},{1,3},{3,5},{5,7},{7,1},{8,10},{10,12},{12... | collective-permute-start | bytes 6152 | tf_op jit(solution)/shard_map/ppermute | solution.py:58
  5.2 16.2 %collective-permute-start.4 = (f32[1,1,16,128]{3,2,1,0:T(8,128)S(1)}, f32[1,1,16,128]{3,2,1,0:T(8,128)S(1)}, u32[]{:S(2)}, u32[]{:S(2)}) collective-permute-start(f32[1,1,16,128]{3,2,1,0:T(8,128)S(1)} %get-tuple-element.104), channel_id=1, source_target_pairs={{8,0},{16,8},{24,16},{32,24},{40,32},{48,40},{56,48},{64,56},{72,6... | collective-permute-start | bytes 24584 | tf_op jit(solution)/shard_map/ppermute | solution.py:60
  11.2 8.2 %collective-permute-start = (f32[1,1,16,128]{3,2,1,0:T(8,128)S(1)}, f32[1,1,16,128]{3,2,1,0:T(8,128)S(1)}, u32[]{:S(2)}, u32[]{:S(2)}) collective-permute-start(f32[1,1,16,128]{3,2,1,0:T(8,128)S(1)} %get-tuple-element.105), channel_id=1, source_target_pairs={{0,8},{8,16},{16,24},{24,32},{32,40},{40,48},{48,56},{56,64},{64,7... | collective-permute-start | bytes 24584 | tf_op jit(solution)/shard_map/ppermute | solution.py:58
  13.4 23.7 %collective-permute-start.8 = (f32[4,18,1]{2,1,0:T(8,128)S(1)}, f32[4,18,1]{2,1,0:T(8,128)S(1)}, u32[]{:S(2)}, u32[]{:S(2)}) collective-permute-start(f32[4,18,1]{2,1,0:T(8,128)S(1)} %get-tuple-element.96), channel_id=1, source_target_pairs={{1,0},{0,1},{3,2},{2,3},{5,4},{4,5},{7,6},{6,7},{9,8},{8,9},{11,10... | collective-permute-start | bytes 872 | tf_op jit(solution)/shard_map/ppermute | solution.py:60
  17.9 19.2 %collective-permute-start.7 = (f32[4,18,1]{2,1,0:T(8,128)S(1)}, f32[4,18,1]{2,1,0:T(8,128)S(1)}, u32[]{:S(2)}, u32[]{:S(2)}) collective-permute-start(f32[4,18,1]{2,1,0:T(8,128)S(1)} %get-tuple-element.97), channel_id=1, source_target_pairs={{0,1},{1,0},{2,3},{3,2},{4,5},{5,4},{6,7},{7,6},{8,9},{9,8},{10,11... | collective-permute-start | bytes 872 | tf_op jit(solution)/shard_map/ppermute | solution.py:58
  19.4 14.0 %collective-permute-start.1 = (f32[1,16,128]{2,1,0:T(8,128)S(1)}, f32[1,16,128]{2,1,0:T(8,128)S(1)}, u32[]{:S(2)}, u32[]{:S(2)}) collective-permute-start(f32[1,16,128]{2,1,0:T(8,128)S(1)} %bitcast.731), channel_id=1, source_target_pairs={{0,2},{2,4},{4,6},{6,0},{1,3},{3,5},{5,7},{7,1},{8,10},{10,12},{12... | collective-permute-start | bytes 24584 | tf_op jit(solution)/shard_map/ppermute | solution.py:41
  19.7 15.3 %collective-permute-start.2 = (f32[1,16,128]{2,1,0:T(8,128)S(1)}, f32[1,16,128]{2,1,0:T(8,128)S(1)}, u32[]{:S(2)}, u32[]{:S(2)}) collective-permute-start(f32[1,16,128]{2,1,0:T(8,128)S(1)} %bitcast.732), channel_id=1, source_target_pairs={{0,6},{2,0},{4,2},{6,4},{1,7},{3,1},{5,3},{7,5},{8,14},{10,8},{12,... | collective-permute-start | bytes 24584 | tf_op jit(solution)/shard_map/ppermute | solution.py:44
  33.4 3.7 %collective-permute-start.3 = (f32[1,16,128]{2,1,0:T(8,128)S(1)}, f32[1,16,128]{2,1,0:T(8,128)S(1)}, u32[]{:S(2)}, u32[]{:S(2)}) collective-permute-start(f32[1,16,128]{2,1,0:T(8,128)S(1)} %collective-permute-done.1), channel_id=1, source_target_pairs={{0,2},{2,4},{4,6},{6,0},{1,3},{3,5},{5,7},{7,1},{8,10},{10,12},{12... | collective-permute-start | bytes 24584 | tf_op jit(solution)/shard_map/ppermute | solution.py:41
  39.3 11.1 %collective-permute-start.13 = (f32[10,1,16,128]{3,2,0,1:T(8,128)S(1)}, f32[10,1,16,128]{3,2,0,1:T(8,128)S(1)}, u32[]{:S(2)}, u32[]{:S(2)}) collective-permute-start(f32[10,1,16,128]{3,2,0,1:T(8,128)S(1)} %get-tuple-element.82), channel_id=1, source_target_pairs={{8,0},{16,8},{24,16},{32,24},{40,32},{48,40},{56,48},{64,56},{72,6... | collective-permute-start | bytes 245768 | tf_op jit(solution)/shard_map/ppermute | solution.py:60
  39.9 7.8 %collective-permute-start.9 = (f32[10,1,16,128]{3,2,0,1:T(8,128)S(1)}, f32[10,1,16,128]{3,2,0,1:T(8,128)S(1)}, u32[]{:S(2)}, u32[]{:S(2)}) collective-permute-start(f32[10,1,16,128]{3,2,0,1:T(8,128)S(1)} %get-tuple-element.83), channel_id=1, source_target_pairs={{0,8},{8,16},{16,24},{24,32},{32,40},{40,48},{48,56},{56,64},{64,7... | collective-permute-start | bytes 245768 | tf_op jit(solution)/shard_map/ppermute | solution.py:58
  47.6 16.0 %collective-permute-start.10 = (f32[10,16,128]{2,1,0:T(8,128)S(1)}, f32[10,16,128]{2,1,0:T(8,128)S(1)}, u32[]{:S(2)}, u32[]{:S(2)}) collective-permute-start(f32[10,16,128]{2,1,0:T(8,128)S(1)} %bitcast.729), channel_id=1, source_target_pairs={{0,2},{2,4},{4,6},{6,0},{1,3},{3,5},{5,7},{7,1},{8,10},{10,12},{12... | collective-permute-start | bytes 245768 | tf_op jit(solution)/shard_map/ppermute | solution.py:41
  50.4 16.3 %collective-permute-start.11 = (f32[10,16,128]{2,1,0:T(8,128)S(1)}, f32[10,16,128]{2,1,0:T(8,128)S(1)}, u32[]{:S(2)}, u32[]{:S(2)}) collective-permute-start(f32[10,16,128]{2,1,0:T(8,128)S(1)} %bitcast.730), channel_id=1, source_target_pairs={{0,6},{2,0},{4,2},{6,4},{1,7},{3,1},{5,3},{7,5},{8,14},{10,8},{12,... | collective-permute-start | bytes 245768 | tf_op jit(solution)/shard_map/ppermute | solution.py:44
  63.7 5.0 %collective-permute-start.12 = (f32[10,16,128]{2,1,0:T(8,128)S(1)}, f32[10,16,128]{2,1,0:T(8,128)S(1)}, u32[]{:S(2)}, u32[]{:S(2)}) collective-permute-start(f32[10,16,128]{2,1,0:T(8,128)S(1)} %collective-permute-done.10), channel_id=1, source_target_pairs={{0,2},{2,4},{4,6},{6,0},{1,3},{3,5},{5,7},{7,1},{8,10},{10,12},{12... | collective-permute-start | bytes 245768 | tf_op jit(solution)/shard_map/ppermute | solution.py:41
  69.0 6.1 %collective-permute-start.14 = (f32[38,6,1,128]{3,0,2,1:T(8,128)S(1)}, f32[38,6,1,128]{3,0,2,1:T(8,128)S(1)}, u32[]{:S(2)}, u32[]{:S(2)}) collective-permute-start(f32[38,6,1,128]{3,0,2,1:T(8,128)S(1)} %copy.222), channel_id=1, source_target_pairs={{0,2},{2,4},{4,6},{6,0},{1,3},{3,5},{5,7},{7,1},{8,10},{10,12},{12... | collective-permute-start | bytes 350216 | tf_op jit(solution)/shard_map/ppermute | solution.py:58
  72.7 6.2 %collective-permute-start.15 = (f32[38,6,1,128]{3,0,2,1:T(8,128)S(1)}, f32[38,6,1,128]{3,0,2,1:T(8,128)S(1)}, u32[]{:S(2)}, u32[]{:S(2)}) collective-permute-start(f32[38,6,1,128]{3,0,2,1:T(8,128)S(1)} %copy.224), channel_id=1, source_target_pairs={{2,0},{4,2},{6,4},{0,6},{3,1},{5,3},{7,5},{1,7},{10,8},{12,10},{14... | collective-permute-start | bytes 350216 | tf_op jit(solution)/shard_map/ppermute | solution.py:60
  85.6 9.1 %collective-permute-start.16 = (f32[38,6,18,1]{0,2,3,1:T(8,128)S(1)}, f32[38,6,18,1]{0,2,3,1:T(8,128)S(1)}, u32[]{:S(2)}, u32[]{:S(2)}) collective-permute-start(f32[38,6,18,1]{0,2,3,1:T(8,128)S(1)} %copy.228), channel_id=1, source_target_pairs={{0,1},{1,0},{2,3},{3,2},{4,5},{5,4},{6,7},{7,6},{8,9},{9,8},{10,11... | collective-permute-start | bytes 49256 | tf_op jit(solution)/shard_map/ppermute | solution.py:58
  93.1 8.3 %collective-permute-start.17 = (f32[38,6,18,1]{0,2,3,1:T(8,128)S(1)}, f32[38,6,18,1]{0,2,3,1:T(8,128)S(1)}, u32[]{:S(2)}, u32[]{:S(2)}) collective-permute-start(f32[38,6,18,1]{0,2,3,1:T(8,128)S(1)} %copy.230), channel_id=1, source_target_pairs={{1,0},{0,1},{3,2},{2,3},{5,4},{4,5},{7,6},{6,7},{9,8},{8,9},{11,10... | collective-permute-start | bytes 49256 | tf_op jit(solution)/shard_map/ppermute | solution.py:60
  105.0 1.8 %copy-start.1 = (f32[38,6,18,1]{3,2,0,1:T(8,128)S(1)}, f32[38,6,18,1]{3,2,0,1:T(8,128)}, u32[]{:S(2)}) copy-start(f32[38,6,18,1]{3,2,0,1:T(8,128)} %copy.231) | copy-start | bytes 49252
  106.8 1.8 %copy-start = (f32[38,6,18,1]{3,2,0,1:T(8,128)S(1)}, f32[38,6,18,1]{3,2,0,1:T(8,128)}, u32[]{:S(2)}) copy-start(f32[38,6,18,1]{3,2,0,1:T(8,128)} %copy.229) | copy-start | bytes 49252
  108.8 1.1 copy-start.4
